TPU v7x, 32 devices: a whole 2x2x4 slice. The times are simulated.
32 devices in a mesh: grp: 1, seq: 4 (over z), dp: 4 (over y, x), head: 2 (over core).
Axes of the slice: x: 2, y: 2, z: 4, core: 2. Of those that a mesh axis runs over, the one named last changes fastest.
Arguments:
- tokens_in: bfloat16 [4, 1024, 4096], P(('grp', 'dp'), 'seq'), may hold values from -6 to 6
- positions: int32 [4, 1024], P(('grp', 'dp'), 'seq'), may hold values from 0 to 1023, as said below
- doc_start: int32 [4, 1024], P(('grp', 'dp'), 'seq'), may hold values from 0 to 1, as said below
- feature_weight: bfloat16 [4096, 4096], P(('seq', 'dp'), 'head'), may hold values from -0.09375 to 0.09375
- state_weight: bfloat16 [4096, 128], P(('seq', 'dp')), may hold values from -0.01171875 to 0.01171875
- step_weight: bfloat16 [4096, 32], P(('seq', 'dp'), 'head'), may hold values from -0.09375 to 0.09375
- step_bias: float32 [32], P('head'), may hold values from -1 to 0.5
- decay_log: float32 [32], P('head')
- skip_gain: float32 [32], P('head'), may hold values from 0.4 to 1.9
- norm_gain: float32 [4096], P('head'), may hold values from 0.5 to 1.5
Outputs:
- mixed: bfloat16 [4, 1024, 4096], P(('grp', 'dp'), 'seq', 'head')
Inputs may be any that keep to these rules, and one draw needn't show every extreme that they name: Each sequence's rows carry every position once. Cut each device's 256 rows into 4 equal slots in order: the positions of slot k all lie in [k * 256, (k + 1) * 256). `doc_start`: position 0 of every sequence holds 1; a sequence holds at most 4 ones.
All inputs are finite; a program needn't handle non-finite values.
Results may differ from a plain program's by a relative error of at most 0.0062.
Values may be sent and summed in bfloat16 or wider, within the bound.
No kernel may reach another device: no remote copies, remote signals or barrier semaphores. Data moves between devices by JAX's collectives and lax.ppermute only.
A program may use at most 128 MiB of HBM per device.

v0:
```python
import jax
import jax.numpy as jnp
from jax import lax
from jax.sharding import PartitionSpec as P

HIGH = lax.Precision.HIGHEST


def carried(gain, state, axis, reverse):
    count = lax.axis_size(axis)
    here = lax.axis_index(axis)
    rows = state.shape[0] * state.shape[1]
    pad = jnp.zeros((8, state.shape[2]), state.dtype).at[0, : gain.shape[0]].set(gain)
    value = jnp.concatenate([state.reshape(rows, -1), pad])

    def shift(x, step):
        if reverse:
            pairs = [(j, j - step) for j in range(step, count)]
            reached = here < count - step
        else:
            pairs = [(j, j + step) for j in range(count - step)]
            reached = here >= step
        return (lax.ppermute(x, axis, pairs), reached)

    value, reached = shift(value, 1)
    value = value.at[rows].set(jnp.where(reached, value[rows], 1.0))
    step = 1
    while step < count:
        earlier, reached = shift(value, step)
        g_early = jnp.where(reached, earlier[rows, : gain.shape[0]], 1.0)
        g_late = value[rows, : gain.shape[0]]
        late = value[:rows].reshape(state.shape)
        merged = g_late[:, None, None] * earlier[:rows].reshape(state.shape) + late
        value = jnp.concatenate(
            [merged.reshape(rows, -1), value[rows:].at[0, : gain.shape[0]].set(g_early * g_late)]
        )
        step *= 2
    return value[:rows].reshape(state.shape)


def per_device(
    tokens_in,
    positions,
    doc_start,
    feature_weight,
    state_weight,
    step_weight,
    step_bias,
    decay_log,
    skip_gain,
    norm_gain,
):
    row_count = tokens_in.shape[1]
    shards = lax.axis_size("seq")
    here = lax.axis_index("seq")
    slot = row_count // shards
    head_count = step_bias.shape[0]
    feat_cols = feature_weight.shape[1]
    head_size = feat_cols // head_count
    state_size = state_weight.shape[1] // 2
    seq_count = lax.axis_size("seq")
    dp_count = lax.axis_size("dp")
    block_rows = feature_weight.shape[0]
    weights = jnp.concatenate([feature_weight, state_weight, step_weight], axis=1)
    gathered = lax.all_gather(weights, "seq", axis=0, tiled=True)
    parts = tokens_in[0].reshape(row_count, seq_count, dp_count, block_rows).transpose(2, 0, 1, 3)
    mine = lax.all_to_all(parts, "dp", 0, 0, tiled=True)
    mine = mine.reshape(dp_count * row_count, seq_count * block_rows)
    partial = jnp.dot(mine, gathered, preferred_element_type=jnp.float32)
    projected = lax.psum_scatter(partial, "dp", scatter_dimension=0, tiled=True)
    projected = projected.astype(jnp.bfloat16).reshape(shards, slot, -1)
    moved = lax.all_to_all(projected, "seq", 0, 0, tiled=True).reshape(row_count, -1)
    moved_positions = lax.all_to_all(
        positions[0].reshape(shards, slot), "seq", 0, 0, tiled=True
    ).reshape(row_count)
    offsets = moved_positions - here * row_count
    inverse = (
        jnp.zeros((row_count,), jnp.int32).at[offsets].set(jnp.arange(row_count, dtype=jnp.int32))
    )
    proj = moved[inverse]
    x_proj = proj[:, :feat_cols]
    bc_proj = proj[:, feat_cols : feat_cols + 2 * state_size]
    step_raw = proj[:, feat_cols + 2 * state_size :]
    b_float = bc_proj[:, :state_size].astype(jnp.float32)
    c_float = bc_proj[:, state_size:].astype(jnp.float32)
    step_size = jax.nn.softplus(step_raw.astype(jnp.float32) + step_bias[None, :])
    log_decay = -jnp.exp(decay_log)[None, :] * step_size
    cum_decay = jnp.cumsum(log_decay, axis=0)
    doc_index = jnp.cumsum(doc_start[0], axis=0)
    scores = jnp.dot(
        bc_proj[:, state_size:], bc_proj[:, :state_size].T, preferred_element_type=jnp.float32
    )
    places = jnp.arange(row_count, dtype=jnp.int32)
    same_doc = (
        (doc_index[:, None] == doc_index[None, :]) & (places[:, None] != places[None, :])
    ).astype(jnp.float32)
    cum_t = cum_decay.T
    step_t = step_size.T
    decay = jnp.exp(-jnp.abs(cum_t[:, :, None] - cum_t[:, None, :])) * same_doc[None]
    mixing = scores[None] * decay * step_t[:, None, :]
    x_heads = x_proj.reshape(row_count, head_count, head_size).astype(jnp.float32)
    y_local = jnp.einsum("hts,shp->thp", mixing, x_heads, precision=HIGH)
    last_doc = (doc_index == doc_index[-1]).astype(jnp.float32)
    first_doc = (doc_index == 0).astype(jnp.float32)
    end_weight = jnp.exp(cum_decay[-1][None, :] - cum_decay) * last_doc[:, None] * step_size
    begin_weight = jnp.exp(cum_decay) * first_doc[:, None] * step_size
    state_end = jnp.einsum("tn,th,thp->hnp", b_float, end_weight, x_heads, precision=HIGH)
    state_begin = jnp.einsum("tn,th,thp->hnp", b_float, begin_weight, x_heads, precision=HIGH)
    carry_gain = jnp.exp(cum_decay[-1]) * (doc_index[-1] == 0)
    prefix = carried(carry_gain, state_end, "seq", False)
    suffix = carried(carry_gain, state_begin, "seq", True)
    left_gate = jnp.exp(cum_decay) * first_doc[:, None]
    right_gate = jnp.exp(cum_decay[-1][None, :] - cum_decay) * last_doc[:, None]
    from_left = jnp.einsum("tn,hnp->thp", c_float, prefix, precision=HIGH)
    from_right = jnp.einsum("tn,hnp->thp", c_float, suffix, precision=HIGH)
    mixer = (
        y_local
        + left_gate[:, :, None] * from_left
        + right_gate[:, :, None] * from_right
        + skip_gain[None, :, None] * x_heads
    )
    mixer_rows = mixer.reshape(row_count, head_count * head_size)
    square_sum = lax.psum(jnp.sum(mixer_rows * mixer_rows, axis=1), "head")
    full_width = mixer_rows.shape[1] * lax.axis_size("head")
    inv_scale = lax.rsqrt(square_sum / full_width + 1e-05)
    return (mixer_rows * inv_scale[:, None] * norm_gain[None, :]).astype(jnp.bfloat16)[None]


def solution(mesh):
    placed = (
        P(("grp", "dp"), "seq", None),
        P(("grp", "dp"), "seq"),
        P(("grp", "dp"), "seq"),
        P(("seq", "dp"), "head"),
        P(("seq", "dp"), None),
        P(("seq", "dp"), "head"),
        P("head"),
        P("head"),
        P("head"),
        P("head"),
    )
    return jax.shard_map(
        per_device,
        mesh=mesh,
        in_specs=placed,
        out_specs=P(("grp", "dp"), "seq", "head"),
        check_vma=False,
    )
```

profile of v0, /device:TPU:0, one launch (start us, length us, event | category | flops | bytes accessed | tf_op | source)
XLA Modules:
  0.0 328.3 jit_solution(13691790862936015671)
XLA Ops:
  7.4 2.4 pad_maximum_fusion
  9.8 3.3 %reshape_squeeze.4 = bf16[256,4,4,256]{3,2,1,0:T(4,128)(2,1)S(1)} reshape(bf16[1,256,4096]{2,1,0:T(8,128)(2,1)} %param.22) | data formatting | bytes 4194304 | tf_op jit(solution)/shard_map/reshape;squeeze | solution.py:66
  13.9 30.4 %all_to_all.19 = bf16[4,256,4,256]{3,2,1,0:T(4,128)(2,1)S(1)} all-to-all(bf16[4,256,4,256]{3,2,1,0:T(4,128)(2,1)S(1)} %bitcast.103), channel_id=1, replica_groups=mesh['grp'=1,'seq'=4,'dp'=4,'head'=2] {'dp'}, dimensions={0} | all-to-all | bytes 4194304 | tf_op jit(solution)/shard_map/all_to_all | solution.py:67
  44.8 57.2 %all-gather.2.cloned.1.call-done = bf16[1024,2192]{1,0:T(8,128)(2,1)} async-done(((bf16[256,2192]{1,0:T(8,128)(2,1)}), bf16[1024,2192]{1,0:T(8,128)(2,1)}) %all-gather.2.cloned.1.call-update) | async-done | bytes 4489232 | tf_op jit(solution)/shard_map/all_gather | solution.py:65
  102.0 10.0 %convolution_bitcast_fusion = f32[1024,2192]{0,1:T(8,128)} fusion(bf16[1024,2192]{1,0:T(8,128)(2,1)} %all-gather.2.cloned.1.call-done, bf16[1024,1024]{1,0:T(8,128)(2,1)S(1)} %bitcast.110), kind=kOutput, calls=%fused_computation.2 | convolution fusion | flops 4596957184 | bytes 15564800 | tf_op jit(solution)/shard_map/dot_general | solution.py:69
  114.0 3.2 all-to-all-start.2
  117.2 84.5 %reduce-scatter.2.cloned.1.call-done = f32[256,2192]{0,1:T(8,128)} async-done(((f32[1024,2192]{0,1:T(8,128)}), f32[256,2192]{0,1:T(8,128)}) %reduce-scatter.2.cloned.1.call-update) | async-done | bytes 2244624 | tf_op jit(solution)/shard_map/reduce_scatter | solution.py:70
  201.7 1.7 convert_element_type.43
  203.5 1.5 copy.77
  205.0 4.6 %all-to-all-start.1 = ((bf16[4,64,2192]{2,1,0:T(8,128)(2,1)}), bf16[4,64,2192]{2,1,0:T(8,128)(2,1)S(1)}, u32[]{:S(2)}, u32[]{:S(2)}) async-start(bf16[4,64,2192]{2,1,0:T(8,128)(2,1)} %bitcast.2), calls=%async_computation.2 | async-start | bytes 2359296 | tf_op jit(solution)/shard_map/all_to_all | solution.py:72
  212.3 1.4 scatter_custom_fusion
  213.7 24.3 %all-to-all-done.1 = bf16[4,64,2192]{2,1,0:T(8,128)(2,1)S(1)} async-done(((bf16[4,64,2192]{2,1,0:T(8,128)(2,1)}), bf16[4,64,2192]{2,1,0:T(8,128)(2,1)S(1)}, u32[]{:S(2)}, u32[]{:S(2)}) %all-to-all-start.1) | async-done | bytes 1122336 | tf_op jit(solution)/shard_map/all_to_all | solution.py:72
  238.0 1.4 gather_fusion
  242.7 1.3 fusion.9
  244.1 1.3 fusion.8
  246.4 1.3 collective-permute-start.3
  247.7 4.6 %collective-permute-start = (f32[1032,128]{1,0:T(8,128)}, f32[1032,128]{1,0:T(8,128)S(1)}, u32[]{:S(2)}, u32[]{:S(2)}) collective-permute-start(f32[1032,128]{1,0:T(8,128)} %get-tuple-element.95), channel_id=1, source_target_pairs={{0,8},{8,16},{16,24},{1,9},{9,17},{17,25},{2,10},{10,18},{18,26},{... | collective-permute-start | bytes 1585160 | tf_op jit(solution)/shard_map/ppermute | solution.py:23
  253.4 8.2 %collective-permute-done.3 = f32[1032,128]{1,0:T(8,128)S(1)} collective-permute-done((f32[1032,128]{1,0:T(8,128)}, f32[1032,128]{1,0:T(8,128)S(1)}, u32[]{:S(2)}, u32[]{:S(2)}) %collective-permute-start.3) | collective-permute-done | bytes 528416 | tf_op jit(solution)/shard_map/ppermute | solution.py:23
  261.6 1.3 collective-permute-start.4
  263.0 5.3 %collective-permute-start.1 = (f32[1032,128]{1,0:T(8,128)S(1)}, f32[1032,128]{1,0:T(8,128)}, u32[]{:S(2)}, u32[]{:S(2)}) collective-permute-start(f32[1032,128]{1,0:T(8,128)S(1)} %scatter.26), channel_id=1, source_target_pairs={{0,8},{8,16},{16,24},{1,9},{9,17},{17,25},{2,10},{10,18},{18,26},{... | collective-permute-start | bytes 1585160 | tf_op jit(solution)/shard_map/ppermute | solution.py:23
  268.3 5.7 %fusion = f32[16,128,256]{2,1,0:T(8,128)} fusion(bf16[256,16,128]{0,2,1:T(8,128)(2,1)S(1)} %bitcast.100, f32[16,256]{1,0:T(8,128)} %get-tuple-element.91, f32[256,256]{1,0:T(8,128)} %fusion.35, f32[16,256]{1,0:T(8,128)} %get-tuple-element.90, f32[256,256]{1,0:T(8,128)S(1)} %fusion.41), kind=kOutput, calls=%fused_computation.3 | convolution fusion | flops 1616904192 | bytes 3702784 | tf_op jit(solution)/shard_map/hts,shp->thp/dot_general | solution.py:102
  274.0 1.8 collective-permute-done.4
  277.8 1.4 multiply_add_fusion.1
  280.1 5.0 %collective-permute-start.2 = (f32[1032,128]{1,0:T(8,128)}, f32[1032,128]{1,0:T(8,128)}, u32[]{:S(2)}, u32[]{:S(2)}) collective-permute-start(f32[1032,128]{1,0:T(8,128)} %pad_maximum_fusion.1), channel_id=1, source_target_pairs={{0,16},{8,24},{1,17},{9,25},{2,18},{10,26},{3,19},{11,27},{4,20},{... | collective-permute-start | bytes 1585160 | tf_op jit(solution)/shard_map/ppermute | solution.py:23
  285.2 1.4 multiply_add_fusion
  286.7 1.3 collective-permute-start.5
  289.3 4.2 %collective-permute-done.2 = f32[1032,128]{1,0:T(8,128)} collective-permute-done((f32[1032,128]{1,0:T(8,128)}, f32[1032,128]{1,0:T(8,128)}, u32[]{:S(2)}, u32[]{:S(2)}) %collective-permute-start.2) | collective-permute-done | bytes 528416 | tf_op jit(solution)/shard_map/ppermute | solution.py:23
  295.8 15.8 %collective-permute-done.5 = f32[1032,128]{1,0:T(8,128)S(1)} collective-permute-done((f32[1032,128]{1,0:T(8,128)S(1)}, f32[1032,128]{1,0:T(8,128)S(1)}, u32[]{:S(2)}, u32[]{:S(2)}) %collective-permute-start.5) | collective-permute-done | bytes 528416 | tf_op jit(solution)/shard_map/ppermute | solution.py:23
  311.7 2.6 multiply_reduce_fusion
  314.4 1.9 copy.88
  316.2 2.4 psum.7
  318.7 2.8 multiply_convert_fusion
  (89 shorter events, 18.3 us)
Async XLA Ops:
  6.5 95.5 %all-gather.2.cloned.1.call-start = ((), (), s32[]{:S(2)}) async-start(), calls=%async_computation.4 | async-start | bytes 5898240 | tf_op jit(solution)/shard_map/all_gather | solution.py:65
  9.7 192.0 %reduce-scatter.2.cloned.1.call-start = ((), (), s32[]{:S(2)}) async-start(), calls=%async_computation.5 | async-start | bytes 11223040 | tf_op jit(solution)/shard_map/reduce_scatter | solution.py:70
  112.0 0.7 copy-start.8
  114.0 91.0 %all-to-all-start.2 = ((s32[4,1,64]{2,1,0:T(1,128)}), s32[4,1,64]{2,1,0:T(1,128)S(1)}, u32[]{:S(2)}, u32[]{:S(2)}) async-start(s32[4,1,64]{2,1,0:T(1,128)} %all_to_all.14), calls=%async_computation.3 | async-start | bytes 4096 | tf_op jit(solution)/shard_map/all_to_all | solution.py:73
  203.5 6.2 %copy-start.9 = (s32[1,256]{1,0:T(1,128)S(1)}, s32[1,256]{1,0:T(1,128)}, u32[]{:S(2)}) copy-start(s32[1,256]{1,0:T(1,128)} %param.24) | copy-start | bytes 3076
  203.5 8.0 %copy-start.11 = (f32[16]{0:T(128)S(1)}, f32[16]{0:T(128)}, u32[]{:S(2)}) copy-start(f32[16]{0:T(128)} %param.29) | copy-start | bytes 196
  205.0 33.0 %all-to-all-start.1 = ((bf16[4,64,2192]{2,1,0:T(8,128)(2,1)}), bf16[4,64,2192]{2,1,0:T(8,128)(2,1)S(1)}, u32[]{:S(2)}, u32[]{:S(2)}) async-start(bf16[4,64,2192]{2,1,0:T(8,128)(2,1)} %bitcast.2), calls=%async_computation.2 | async-start | bytes 2359296 | tf_op jit(solution)/shard_map/all_to_all | solution.py:72
  239.4 55.2 %copy-start = (bf16[256,2192]{1,0:T(8,128)(2,1)}, bf16[256,2192]{1,0:T(8,128)(2,1)S(1)}, u32[]{:S(2)}) copy-start(bf16[256,2192]{1,0:T(8,128)(2,1)S(1)} %gather_fusion) | copy-start | bytes 3366916
  239.4 0.7 copy-start.7
  246.4 15.1 %collective-permute-start.3 = (f32[1032,128]{1,0:T(8,128)}, f32[1032,128]{1,0:T(8,128)S(1)}, u32[]{:S(2)}, u32[]{:S(2)}) collective-permute-start(f32[1032,128]{1,0:T(8,128)} %get-tuple-element.94), channel_id=1, source_target_pairs={{8,0},{16,8},{24,16},{9,1},{17,9},{25,17},{10,2},{18,10},{26,18},{... | collective-permute-start | bytes 1585160 | tf_op jit(solution)/shard_map/ppermute | solution.py:23
  247.7 15.2 %collective-permute-start = (f32[1032,128]{1,0:T(8,128)}, f32[1032,128]{1,0:T(8,128)S(1)}, u32[]{:S(2)}, u32[]{:S(2)}) collective-permute-start(f32[1032,128]{1,0:T(8,128)} %get-tuple-element.95), channel_id=1, source_target_pairs={{0,8},{8,16},{16,24},{1,9},{9,17},{17,25},{2,10},{10,18},{18,26},{... | collective-permute-start | bytes 1585160 | tf_op jit(solution)/shard_map/ppermute | solution.py:23
  261.6 12.4 %copy-start.3 = (f32[1032,128]{1,0:T(8,128)}, f32[1032,128]{1,0:T(8,128)S(1)}, u32[]{:S(2)}) copy-start(f32[1032,128]{1,0:T(8,128)S(1)} %scatter.30) | copy-start | bytes 1585156
  261.6 14.2 %collective-permute-start.4 = (f32[1032,128]{1,0:T(8,128)S(1)}, f32[1032,128]{1,0:T(8,128)}, u32[]{:S(2)}, u32[]{:S(2)}) collective-permute-start(f32[1032,128]{1,0:T(8,128)S(1)} %scatter.30), channel_id=1, source_target_pairs={{8,0},{16,8},{24,16},{9,1},{17,9},{25,17},{10,2},{18,10},{26,18},{... | collective-permute-start | bytes 1585160 | tf_op jit(solution)/shard_map/ppermute | solution.py:23
  263.0 11.0 %copy-start.2 = (f32[1032,128]{1,0:T(8,128)}, f32[1032,128]{1,0:T(8,128)S(1)}, u32[]{:S(2)}) copy-start(f32[1032,128]{1,0:T(8,128)S(1)} %scatter.26) | copy-start | bytes 1585156
  263.0 13.9 %collective-permute-start.1 = (f32[1032,128]{1,0:T(8,128)S(1)}, f32[1032,128]{1,0:T(8,128)}, u32[]{:S(2)}, u32[]{:S(2)}) collective-permute-start(f32[1032,128]{1,0:T(8,128)S(1)} %scatter.26), channel_id=1, source_target_pairs={{0,8},{8,16},{16,24},{1,9},{9,17},{17,25},{2,10},{10,18},{18,26},{... | collective-permute-start | bytes 1585160 | tf_op jit(solution)/shard_map/ppermute | solution.py:23
  280.1 13.4 %collective-permute-start.2 = (f32[1032,128]{1,0:T(8,128)}, f32[1032,128]{1,0:T(8,128)}, u32[]{:S(2)}, u32[]{:S(2)}) collective-permute-start(f32[1032,128]{1,0:T(8,128)} %pad_maximum_fusion.1), channel_id=1, source_target_pairs={{0,16},{8,24},{1,17},{9,25},{2,18},{10,26},{3,19},{11,27},{4,20},{... | collective-permute-start | bytes 1585160 | tf_op jit(solution)/shard_map/ppermute | solution.py:23
  286.7 25.0 %collective-permute-start.5 = (f32[1032,128]{1,0:T(8,128)S(1)}, f32[1032,128]{1,0:T(8,128)S(1)}, u32[]{:S(2)}, u32[]{:S(2)}) collective-permute-start(f32[1032,128]{1,0:T(8,128)S(1)} %pad_maximum_fusion.2), channel_id=1, source_target_pairs={{16,0},{24,8},{17,1},{25,9},{18,2},{26,10},{19,3},{27,11},{20,4},{... | collective-permute-start | bytes 1585160 | tf_op jit(solution)/shard_map/ppermute | solution.py:23
  294.6 17.1 %copy-start.1 = (f32[16,128,256]{2,1,0:T(8,128)S(1)}, f32[16,128,256]{2,1,0:T(8,128)}, u32[]{:S(2)}) copy-start(f32[16,128,256]{2,1,0:T(8,128)} %fusion) | copy-start | bytes 6291460
  294.6 17.1 %copy-start.4 = (f32[256,16]{0,1:T(8,128)S(1)}, f32[256,16]{0,1:T(8,128)}, u32[]{:S(2)}) copy-start(f32[256,16]{0,1:T(8,128)} %get-tuple-element.74) | copy-start | bytes 49156
  294.6 17.1 %copy-start.5 = (f32[256,16]{0,1:T(8,128)S(1)}, f32[256,16]{0,1:T(8,128)}, u32[]{:S(2)}) copy-start(f32[256,16]{0,1:T(8,128)} %get-tuple-element.86) | copy-start | bytes 49156
  294.6 17.1 %copy-start.10 = (f32[16]{0:T(128)S(1)}, f32[16]{0:T(128)}, u32[]{:S(2)}) copy-start(f32[16]{0:T(128)} %param.30) | copy-start | bytes 196
  314.4 4.3 %copy-start.6 = (f32[2048]{0:T(1024)S(1)}, f32[2048]{0:T(1024)}, u32[]{:S(2)}) copy-start(f32[2048]{0:T(1024)} %param.31) | copy-start | bytes 24580
Sparse Core Ops, SparseCore 0:
  9.9 92.0 all-gather.1
  112.1 89.5 reduce-scatter.1
where the time goes:
time: 329 us; the launch traced here: 328 us
  waiting for transfers between devices  196 us (60%)
  blocking collectives  32.8 us (10%)
  starting transfers between devices  26.7 us (8%)
  matrix products  22.3 us (7%)
  other arithmetic  19.3 us (6%)
  local copies, waits for them, and re-layouts  16.5 us (5%)
  between operations  14.4 us (4%)
    reduce_scatter x1, waiting for transfers between devices, per_device(): projected = lax.psum_scatter(partial, 'dp', scatter_dimension=0, tiled=True)  84.5 us
    all_gather x1, waiting for transfers between devices, per_device(): gathered = lax.all_gather(weights, 'seq', axis=0, tiled=True)  57.2 us
    all_to_all x1, blocking collectives, per_device(): mine = lax.all_to_all(parts, 'dp', 0, 0, tiled=True)  30.4 us
    ppermute x6, waiting for transfers between devices, shift(): return (lax.ppermute(x, axis, pairs), reached)  30.3 us
    all_to_all x1, waiting for transfers between devices, per_device(): lax.all_to_all(projected, 'seq', 0, 0, tiled=True).reshape(row_count, -1)  24.3 us
    ppermute x6, starting transfers between devices, shift(): return (lax.ppermute(x, axis, pairs), reached)  18.8 us
    dot_general x1, matrix products, per_device(): partial = jnp.dot(mine, gathered, preferred_element_type=jnp.float32)  9.96 us
  transfers between devices with their start and end apart: 10, of which 8 were waited for; matrix products, arithmetic and copies ran while one was open for 8% of the time, Pallas kernels for 0%

commit v1 on v0

--- a/solution.py
+++ b/solution.py
@@ -1,9 +1,42 @@
+import functools
 import jax
 import jax.numpy as jnp
 from jax import lax
 from jax.sharding import PartitionSpec as P
 
 HIGH = lax.Precision.HIGHEST
+
+
+def _balance_panel(vals, array_axis, chunk):
+    extra = vals.shape
+    block_out = vals.reshape(
+        *extra[:array_axis], chunk, extra[array_axis] // chunk, *extra[array_axis + 1 :]
+    )
+    return jnp.moveaxis(block_out, array_axis, 0)
+
+
+def skins_find(u_in, d0):
+    carry = list(u_in.shape[1:])
+    carry[d0] *= u_in.shape[0]
+    return jnp.moveaxis(u_in, 0, d0).reshape(carry)
+
+
+def turn_racks(xs, comm_axis, content, q_in):
+    newest = lax.axis_index(comm_axis)
+    local_out = lax.axis_size(comm_axis)
+    big, raw_out = (local_out, newest)
+    arr_out = _balance_panel(xs, content, big)
+    sheets = [arr_out[raw_out]]
+    for jj in tuple(range(1, big)):
+        current_value = arr_out[raw_out ^ jj]
+        arr_now = lax.ppermute(current_value, comm_axis, [(to_i, to_i ^ jj) for to_i in range(big)])
+        sheets.append(arr_now)
+    mid_arr = jnp.stack(sheets, axis=0)
+    arr_out = mid_arr[raw_out ^ jnp.arange(big)]
+    return skins_find(arr_out, q_in)
+
+
+step_on_things_for = functools.partial(turn_racks, comm_axis="seq", content=0, q_in=0)
 
 
 def carried(gain, state, axis, reverse):
@@ -69,7 +102,7 @@
     partial = jnp.dot(mine, gathered, preferred_element_type=jnp.float32)
     projected = lax.psum_scatter(partial, "dp", scatter_dimension=0, tiled=True)
     projected = projected.astype(jnp.bfloat16).reshape(shards, slot, -1)
-    moved = lax.all_to_all(projected, "seq", 0, 0, tiled=True).reshape(row_count, -1)
+    moved = step_on_things_for(projected).reshape(row_count, -1)
     moved_positions = lax.all_to_all(
         positions[0].reshape(shards, slot), "seq", 0, 0, tiled=True
     ).reshape(row_count)

time: 329 us -> 325 us (0.988)
  waiting for transfers between devices: 196 us -> 192 us
    all_to_all x1 -> x0, waiting for transfers between devices: 24.3 us -> none  [per_device(): lax.all_to_all(projected, 'seq', 0, 0, tiled=True).reshape(row_count, -1)]
    ppermute x0 -> x3, waiting for transfers between devices: none -> 24.1 us  [turn_racks(): lax.ppermute(current_value, comm_axis, [(to_i, to_i ^ jj) for to_i in ran...]
    reduce_scatter x1, waiting for transfers between devices: 84.5 us -> 77.5 us  [per_device(): projected = lax.psum_scatter(partial, 'dp', scatter_dimension=0, tiled=True)]
    all_to_all x1 -> x0, starting transfers between devices: 4.59 us -> none  [per_device(): lax.all_to_all(projected, 'seq', 0, 0, tiled=True).reshape(row_count, -1)]
    ppermute x0 -> x3, starting transfers between devices: none -> 4.45 us  [turn_racks(): lax.ppermute(current_value, comm_axis, [(to_i, to_i ^ jj) for to_i in ran...]
  transfers between devices with their start and end apart: 10 -> 12, of which waited for: 8 -> 10; matrix products, arithmetic and copies ran while one was open for 8% -> 7% of each run, Pallas kernels for 0% -> 0%
where the time goes in v1:
time: 325 us; the launch traced here: 324 us
  waiting for transfers between devices  192 us (59%)
  blocking collectives  32.8 us (10%)
  starting transfers between devices  26.7 us (8%)
  matrix products  22.3 us (7%)
  other arithmetic  19.4 us (6%)
  local copies, waits for them, and re-layouts  16.4 us (5%)
  between operations  14.4 us (4%)
    reduce_scatter x1, waiting for transfers between devices, per_device(): projected = lax.psum_scatter(partial, 'dp', scatter_dimension=0, tiled=True)  77.5 us
    all_gather x1, waiting for transfers between devices, per_device(): gathered = lax.all_gather(weights, 'seq', axis=0, tiled=True)  57.2 us
    ppermute x6, waiting for transfers between devices, shift(): return (lax.ppermute(x, axis, pairs), reached)  30.4 us
    all_to_all x1, blocking collectives, per_device(): mine = lax.all_to_all(parts, 'dp', 0, 0, tiled=True)  30.4 us
    ppermute x3, waiting for transfers between devices, turn_racks(): lax.ppermute(current_value, comm_axis, [(to_i, to_i ^ jj) for to_i in ran...  24.1 us
    ppermute x6, starting transfers between devices, shift(): return (lax.ppermute(x, axis, pairs), reached)  19 us
    dot_general x1, matrix products, per_device(): partial = jnp.dot(mine, gathered, preferred_element_type=jnp.float32)  9.95 us
  transfers between devices with their start and end apart: 12, of which 10 were waited for; matrix products, arithmetic and copies ran while one was open for 7% of the time, Pallas kernels for 0%

profile of v1, /device:TPU:0, one launch (start us, length us, event | category | flops | bytes accessed | tf_op | source)
XLA Modules:
  0.0 324.2 jit_solution(13349305864751051352)
XLA Ops:
  7.4 2.4 pad_maximum_fusion
  9.8 3.3 %reshape_squeeze.4 = bf16[256,4,4,256]{3,2,1,0:T(4,128)(2,1)S(1)} reshape(bf16[1,256,4096]{2,1,0:T(8,128)(2,1)} %param.22) | data formatting | bytes 4194304 | tf_op jit(solution)/shard_map/reshape;squeeze | solution.py:99
  14.0 30.4 %all_to_all.14 = bf16[4,256,4,256]{3,2,1,0:T(4,128)(2,1)S(1)} all-to-all(bf16[4,256,4,256]{3,2,1,0:T(4,128)(2,1)S(1)} %bitcast.122), channel_id=1, replica_groups=mesh['grp'=1,'seq'=4,'dp'=4,'head'=2] {'dp'}, dimensions={0} | all-to-all | bytes 4194304 | tf_op jit(solution)/shard_map/all_to_all | solution.py:100
  44.8 57.2 %all-gather.2.cloned.1.call-done = bf16[1024,2192]{1,0:T(8,128)(2,1)} async-done(((bf16[256,2192]{1,0:T(8,128)(2,1)}), bf16[1024,2192]{1,0:T(8,128)(2,1)}) %all-gather.2.cloned.1.call-update) | async-done | bytes 4489232 | tf_op jit(solution)/shard_map/all_gather | solution.py:98
  102.0 10.0 %convolution_bitcast_fusion = f32[1024,2192]{0,1:T(8,128)} fusion(bf16[1024,2192]{1,0:T(8,128)(2,1)} %all-gather.2.cloned.1.call-done, bf16[1024,1024]{1,0:T(8,128)(2,1)S(1)} %bitcast.130), kind=kOutput, calls=%fused_computation.3 | convolution fusion | flops 4596957184 | bytes 15564800 | tf_op jit(solution)/shard_map/dot_general | solution.py:102
  114.0 3.2 all-to-all-start.1
  119.7 2.9 all-to-all-done.1
  122.8 1.4 scatter_custom_fusion
  124.2 77.5 %reduce-scatter.2.cloned.1.call-done = f32[256,2192]{0,1:T(8,128)} async-done(((f32[1024,2192]{0,1:T(8,128)}), f32[256,2192]{0,1:T(8,128)}) %reduce-scatter.2.cloned.1.call-update) | async-done | bytes 2244624 | tf_op jit(solution)/shard_map/reduce_scatter | solution.py:103
  201.7 1.7 convert_element_type.43
  204.3 3.4 %collective-permute-start.2 = (bf16[1,64,2192]{2,1,0:T(8,128)(2,1)S(1)}, bf16[1,64,2192]{2,1,0:T(8,128)(2,1)S(1)}, u32[]{:S(2)}, u32[]{:S(2)}) collective-permute-start(bf16[1,64,2192]{2,1,0:T(8,128)(2,1)S(1)} %get-tuple-element.80), channel_id=1, source_target_pairs={{0,24},{8,16},{16,8},{24,0},{1,25},{9,17},{17,9},{25,1},{2,26},{10... | collective-permute-start | bytes 841736 | tf_op jit(solution)/shard_map/ppermute | solution.py:32
  208.8 7.4 %collective-permute-done.2 = bf16[1,64,2192]{2,1,0:T(8,128)(2,1)S(1)} collective-permute-done((bf16[1,64,2192]{2,1,0:T(8,128)(2,1)S(1)}, bf16[1,64,2192]{2,1,0:T(8,128)(2,1)S(1)}, u32[]{:S(2)}, u32[]{:S(2)}) %collective-permute-start.2) | collective-permute-done | bytes 280608 | tf_op jit(solution)/shard_map/ppermute | solution.py:32
  216.1 16.7 %collective-permute-done.1 = bf16[1,64,2192]{2,1,0:T(8,128)(2,1)S(1)} collective-permute-done((bf16[1,64,2192]{2,1,0:T(8,128)(2,1)S(1)}, bf16[1,64,2192]{2,1,0:T(8,128)(2,1)S(1)}, u32[]{:S(2)}, u32[]{:S(2)}) %collective-permute-start.1) | collective-permute-done | bytes 280608 | tf_op jit(solution)/shard_map/ppermute | solution.py:32
  233.6 1.4 gather_fusion.1
  238.4 1.3 fusion.9
  239.7 1.3 fusion.8
  243.4 4.6 %collective-permute-start.3 = (f32[1032,128]{1,0:T(8,128)}, f32[1032,128]{1,0:T(8,128)S(1)}, u32[]{:S(2)}, u32[]{:S(2)}) collective-permute-start(f32[1032,128]{1,0:T(8,128)} %get-tuple-element.99), channel_id=1, source_target_pairs={{0,8},{8,16},{16,24},{1,9},{9,17},{17,25},{2,10},{10,18},{18,26},{... | collective-permute-start | bytes 1585160 | tf_op jit(solution)/shard_map/ppermute | solution.py:56
  249.0 8.2 %collective-permute-done.6 = f32[1032,128]{1,0:T(8,128)S(1)} collective-permute-done((f32[1032,128]{1,0:T(8,128)}, f32[1032,128]{1,0:T(8,128)S(1)}, u32[]{:S(2)}, u32[]{:S(2)}) %collective-permute-start.6) | collective-permute-done | bytes 528416 | tf_op jit(solution)/shard_map/ppermute | solution.py:56
  257.3 1.3 collective-permute-start.7
  258.6 5.5 %collective-permute-start.4 = (f32[1032,128]{1,0:T(8,128)S(1)}, f32[1032,128]{1,0:T(8,128)}, u32[]{:S(2)}, u32[]{:S(2)}) collective-permute-start(f32[1032,128]{1,0:T(8,128)S(1)} %scatter.26), channel_id=1, source_target_pairs={{0,8},{8,16},{16,24},{1,9},{9,17},{17,25},{2,10},{10,18},{18,26},{... | collective-permute-start | bytes 1585160 | tf_op jit(solution)/shard_map/ppermute | solution.py:56
  264.2 5.7 %fusion = f32[16,128,256]{2,1,0:T(8,128)} fusion(bf16[256,16,128]{0,2,1:T(8,128)(2,1)S(1)} %bitcast.119, f32[16,256]{1,0:T(8,128)} %get-tuple-element.95, f32[256,256]{1,0:T(8,128)} %fusion.35, f32[16,256]{1,0:T(8,128)} %get-tuple-element.94, f32[256,256]{1,0:T(8,128)S(1)} %fusion.41), kind=kOutput, calls=%fused_computation.4 | convolution fusion | flops 1616904192 | bytes 3702784 | tf_op jit(solution)/shard_map/hts,shp->thp/dot_general | solution.py:135
  269.9 1.6 collective-permute-done.7
  273.5 1.4 multiply_add_fusion.1
  275.8 5.0 %collective-permute-start.5 = (f32[1032,128]{1,0:T(8,128)}, f32[1032,128]{1,0:T(8,128)}, u32[]{:S(2)}, u32[]{:S(2)}) collective-permute-start(f32[1032,128]{1,0:T(8,128)} %pad_maximum_fusion.1), channel_id=1, source_target_pairs={{0,16},{8,24},{1,17},{9,25},{2,18},{10,26},{3,19},{11,27},{4,20},{... | collective-permute-start | bytes 1585160 | tf_op jit(solution)/shard_map/ppermute | solution.py:56
  280.9 1.4 multiply_add_fusion
  282.4 1.3 collective-permute-start.8
  285.0 4.2 %collective-permute-done.5 = f32[1032,128]{1,0:T(8,128)} collective-permute-done((f32[1032,128]{1,0:T(8,128)}, f32[1032,128]{1,0:T(8,128)}, u32[]{:S(2)}, u32[]{:S(2)}) %collective-permute-start.5) | collective-permute-done | bytes 528416 | tf_op jit(solution)/shard_map/ppermute | solution.py:56
  291.5 16.0 %collective-permute-done.8 = f32[1032,128]{1,0:T(8,128)S(1)} collective-permute-done((f32[1032,128]{1,0:T(8,128)S(1)}, f32[1032,128]{1,0:T(8,128)S(1)}, u32[]{:S(2)}, u32[]{:S(2)}) %collective-permute-start.8) | collective-permute-done | bytes 528416 | tf_op jit(solution)/shard_map/ppermute | solution.py:56
  307.6 2.6 multiply_reduce_fusion
  310.3 1.9 copy.100
  312.1 2.4 psum.7
  314.6 2.8 multiply_convert_fusion
  (98 shorter events, 22.2 us)
Async XLA Ops:
  6.5 95.5 %all-gather.2.cloned.1.call-start = ((), (), s32[]{:S(2)}) async-start(), calls=%async_computation.3 | async-start | bytes 5898240 | tf_op jit(solution)/shard_map/all_gather | solution.py:98
  9.8 192.0 %reduce-scatter.2.cloned.1.call-start = ((), (), s32[]{:S(2)}) async-start(), calls=%async_computation.4 | async-start | bytes 11223040 | tf_op jit(solution)/shard_map/reduce_scatter | solution.py:103
  112.0 0.7 copy-start.8
  112.0 5.2 %copy-start.9 = (s32[1,256]{1,0:T(1,128)S(1)}, s32[1,256]{1,0:T(1,128)}, u32[]{:S(2)}) copy-start(s32[1,256]{1,0:T(1,128)} %param.24) | copy-start | bytes 3076
  112.0 6.5 %copy-start.11 = (f32[16]{0:T(128)S(1)}, f32[16]{0:T(128)}, u32[]{:S(2)}) copy-start(f32[16]{0:T(128)} %param.29) | copy-start | bytes 196
  114.0 8.7 %all-to-all-start.1 = ((s32[4,1,64]{2,1,0:T(1,128)}), s32[4,1,64]{2,1,0:T(1,128)S(1)}, u32[]{:S(2)}, u32[]{:S(2)}) async-start(s32[4,1,64]{2,1,0:T(1,128)} %all_to_all.10), calls=%async_computation.2 | async-start | bytes 4096 | tf_op jit(solution)/shard_map/all_to_all | solution.py:106
  204.3 11.8 %collective-permute-start.2 = (bf16[1,64,2192]{2,1,0:T(8,128)(2,1)S(1)}, bf16[1,64,2192]{2,1,0:T(8,128)(2,1)S(1)}, u32[]{:S(2)}, u32[]{:S(2)}) collective-permute-start(bf16[1,64,2192]{2,1,0:T(8,128)(2,1)S(1)} %get-tuple-element.80), channel_id=1, source_target_pairs={{0,24},{8,16},{16,8},{24,0},{1,25},{9,17},{17,9},{25,1},{2,26},{10... | collective-permute-start | bytes 841736 | tf_op jit(solution)/shard_map/ppermute | solution.py:32
  207.7 25.1 %collective-permute-start.1 = (bf16[1,64,2192]{2,1,0:T(8,128)(2,1)S(1)}, bf16[1,64,2192]{2,1,0:T(8,128)(2,1)S(1)}, u32[]{:S(2)}, u32[]{:S(2)}) collective-permute-start(bf16[1,64,2192]{2,1,0:T(8,128)(2,1)S(1)} %get-tuple-element.81), channel_id=1, source_target_pairs={{0,16},{8,24},{16,0},{24,8},{1,17},{9,25},{17,1},{25,9},{2,18},{10... | collective-permute-start | bytes 841736 | tf_op jit(solution)/shard_map/ppermute | solution.py:32
  207.7 25.1 %collective-permute-start = (bf16[1,64,2192]{2,1,0:T(8,128)(2,1)S(1)}, bf16[1,64,2192]{2,1,0:T(8,128)(2,1)S(1)}, u32[]{:S(2)}, u32[]{:S(2)}) collective-permute-start(bf16[1,64,2192]{2,1,0:T(8,128)(2,1)S(1)} %get-tuple-element.82), channel_id=1, source_target_pairs={{0,8},{8,0},{16,24},{24,16},{1,9},{9,1},{17,25},{25,17},{2,10},{10... | collective-permute-start | bytes 841736 | tf_op jit(solution)/shard_map/ppermute | solution.py:32
  235.1 55.2 %copy-start = (bf16[256,2192]{1,0:T(8,128)(2,1)}, bf16[256,2192]{1,0:T(8,128)(2,1)S(1)}, u32[]{:S(2)}) copy-start(bf16[256,2192]{1,0:T(8,128)(2,1)S(1)} %gather_fusion.1) | copy-start | bytes 3366916
  235.1 0.7 copy-start.7
  242.1 15.2 %collective-permute-start.6 = (f32[1032,128]{1,0:T(8,128)}, f32[1032,128]{1,0:T(8,128)S(1)}, u32[]{:S(2)}, u32[]{:S(2)}) collective-permute-start(f32[1032,128]{1,0:T(8,128)} %get-tuple-element.98), channel_id=1, source_target_pairs={{8,0},{16,8},{24,16},{9,1},{17,9},{25,17},{10,2},{18,10},{26,18},{... | collective-permute-start | bytes 1585160 | tf_op jit(solution)/shard_map/ppermute | solution.py:56
  243.4 15.2 %collective-permute-start.3 = (f32[1032,128]{1,0:T(8,128)}, f32[1032,128]{1,0:T(8,128)S(1)}, u32[]{:S(2)}, u32[]{:S(2)}) collective-permute-start(f32[1032,128]{1,0:T(8,128)} %get-tuple-element.99), channel_id=1, source_target_pairs={{0,8},{8,16},{16,24},{1,9},{9,17},{17,25},{2,10},{10,18},{18,26},{... | collective-permute-start | bytes 1585160 | tf_op jit(solution)/shard_map/ppermute | solution.py:56
  257.3 12.6 %copy-start.3 = (f32[1032,128]{1,0:T(8,128)}, f32[1032,128]{1,0:T(8,128)S(1)}, u32[]{:S(2)}) copy-start(f32[1032,128]{1,0:T(8,128)S(1)} %scatter.30) | copy-start | bytes 1585156
  257.3 14.2 %collective-permute-start.7 = (f32[1032,128]{1,0:T(8,128)S(1)}, f32[1032,128]{1,0:T(8,128)}, u32[]{:S(2)}, u32[]{:S(2)}) collective-permute-start(f32[1032,128]{1,0:T(8,128)S(1)} %scatter.30), channel_id=1, source_target_pairs={{8,0},{16,8},{24,16},{9,1},{17,9},{25,17},{10,2},{18,10},{26,18},{... | collective-permute-start | bytes 1585160 | tf_op jit(solution)/shard_map/ppermute | solution.py:56
  258.6 11.2 %copy-start.2 = (f32[1032,128]{1,0:T(8,128)}, f32[1032,128]{1,0:T(8,128)S(1)}, u32[]{:S(2)}) copy-start(f32[1032,128]{1,0:T(8,128)S(1)} %scatter.26) | copy-start | bytes 1585156
  258.6 14.0 %collective-permute-start.4 = (f32[1032,128]{1,0:T(8,128)S(1)}, f32[1032,128]{1,0:T(8,128)}, u32[]{:S(2)}, u32[]{:S(2)}) collective-permute-start(f32[1032,128]{1,0:T(8,128)S(1)} %scatter.26), channel_id=1, source_target_pairs={{0,8},{8,16},{16,24},{1,9},{9,17},{17,25},{2,10},{10,18},{18,26},{... | collective-permute-start | bytes 1585160 | tf_op jit(solution)/shard_map/ppermute | solution.py:56
  275.8 13.4 %collective-permute-start.5 = (f32[1032,128]{1,0:T(8,128)}, f32[1032,128]{1,0:T(8,128)}, u32[]{:S(2)}, u32[]{:S(2)}) collective-permute-start(f32[1032,128]{1,0:T(8,128)} %pad_maximum_fusion.1), channel_id=1, source_target_pairs={{0,16},{8,24},{1,17},{9,25},{2,18},{10,26},{3,19},{11,27},{4,20},{... | collective-permute-start | bytes 1585160 | tf_op jit(solution)/shard_map/ppermute | solution.py:56
  282.4 25.2 %collective-permute-start.8 = (f32[1032,128]{1,0:T(8,128)S(1)}, f32[1032,128]{1,0:T(8,128)S(1)}, u32[]{:S(2)}, u32[]{:S(2)}) collective-permute-start(f32[1032,128]{1,0:T(8,128)S(1)} %pad_maximum_fusion.2), channel_id=1, source_target_pairs={{16,0},{24,8},{17,1},{25,9},{18,2},{26,10},{19,3},{27,11},{20,4},{... | collective-permute-start | bytes 1585160 | tf_op jit(solution)/shard_map/ppermute | solution.py:56
  290.3 17.3 %copy-start.1 = (f32[16,128,256]{2,1,0:T(8,128)S(1)}, f32[16,128,256]{2,1,0:T(8,128)}, u32[]{:S(2)}) copy-start(f32[16,128,256]{2,1,0:T(8,128)} %fusion) | copy-start | bytes 6291460
  290.3 17.3 %copy-start.4 = (f32[256,16]{0,1:T(8,128)S(1)}, f32[256,16]{0,1:T(8,128)}, u32[]{:S(2)}) copy-start(f32[256,16]{0,1:T(8,128)} %get-tuple-element.74) | copy-start | bytes 49156
  290.3 17.3 %copy-start.5 = (f32[256,16]{0,1:T(8,128)S(1)}, f32[256,16]{0,1:T(8,128)}, u32[]{:S(2)}) copy-start(f32[256,16]{0,1:T(8,128)} %get-tuple-element.90) | copy-start | bytes 49156
  290.3 17.3 %copy-start.10 = (f32[16]{0:T(128)S(1)}, f32[16]{0:T(128)}, u32[]{:S(2)}) copy-start(f32[16]{0:T(128)} %param.30) | copy-start | bytes 196
  310.2 4.3 %copy-start.6 = (f32[2048]{0:T(1024)S(1)}, f32[2048]{0:T(1024)}, u32[]{:S(2)}) copy-start(f32[2048]{0:T(1024)} %param.31) | copy-start | bytes 24580
Sparse Core Ops, SparseCore 0:
  9.9 92.0 all-gather.1
  112.1 89.5 reduce-scatter.1
